TPU v7x, 32 devices: a whole 2x2x4 slice. The times are simulated.
32 devices in a mesh: member: 1, lat: 32 (over z, y, x, core).
Axes of the slice: x: 2, y: 2, z: 4, core: 2. Of those that a mesh axis runs over, the one named last changes fastest.
Arguments:
- spectral: bfloat16 [512, 512, 256], P(('member', 'lat')), may hold values from -6 to 6
- lat_basis: bfloat16 [512, 512, 192], P('lat'), may hold values from -0.0078125 to 0.0078125
- block_order: int32 [128], replicated, may hold values from 0 to 127, each once
- in_weight: bfloat16 [128, 1024], replicated, may hold values from -0.5 to 0.5
- in_bias: float32 [1024], replicated, may hold values from -3 to 3
- out_weight: bfloat16 [1024, 128], replicated, may hold values from -0.1875 to 0.1875
- col_gain: float32 [128], replicated, may hold values from 0.5 to 2
- damping: float32 [128], replicated, may hold values from 0.2 to 2
Outputs:
- tendency: float32 [512, 512, 256], P(('member', 'lat'))
Inputs may be any that keep to these rules, and one draw needn't show every extreme that they name: `block_order`: each wavenumber block appears exactly once.
All inputs are finite; a program needn't handle non-finite values.
Results may differ from a plain program's by a relative error of at most 0.004.
The roundings to bfloat16 on the way count: a program that leaves them out, or rounds other values in their place, can miss the bound.
Values may be sent and summed in bfloat16 or wider, within the bound.
No kernel may reach another device: no remote copies, remote signals or barrier semaphores. Data moves between devices by JAX's collectives and lax.ppermute only.
A program may use at most 128 MiB of HBM per device.

v0:
```python
import math
import jax
import jax.numpy as jnp
from jax import lax
from jax.sharding import PartitionSpec as P

NN = 512
NLON = 1536
MB = 4


def wavenumbers(block_order, slot_count):
    slot_ids = jnp.arange(slot_count, dtype=jnp.int32)
    blocks = block_order.shape[0]
    matches = (slot_ids // MB)[:, None] == jnp.arange(blocks, dtype=jnp.int32)[None, :]
    chosen = jnp.sum(jnp.where(matches, block_order[None, :], 0), axis=1)
    return chosen * MB + slot_ids % MB


def lon_table(wave_all):
    longitude = jnp.arange(NLON, dtype=jnp.int32)
    phase_index = wave_all[:, None] * longitude[None, :] % NLON
    angles = phase_index.astype(jnp.float32) * (2.0 * math.pi / NLON)
    return jnp.concatenate([jnp.cos(angles), jnp.sin(angles)], axis=0).astype(jnp.bfloat16)


def lat_weights(first_lat, lat_count, lat_total):
    latitude = (first_lat + jnp.arange(lat_count, dtype=jnp.int32)).astype(jnp.float32)
    return jnp.cos(math.pi * ((latitude + 0.5) / lat_total - 0.5))


def on_device(spectral, lat_basis, block_order, in_weight, in_bias, out_weight, col_gain, damping):
    devices = lax.axis_size("lat")
    my_index = lax.axis_index("lat")
    row_count = spectral.shape[0]
    degrees = spectral.shape[1]
    chan_width = spectral.shape[2]
    chan_count = chan_width // 2
    half_lat = lat_basis.shape[2]
    lat_total = 2 * half_lat
    lat_local = lat_total // devices
    wave_total = row_count * devices
    wave_all = wavenumbers(block_order, wave_total)
    wave_own = lax.dynamic_slice_in_dim(wave_all, my_index * row_count, row_count)
    degree = jnp.arange(degrees, dtype=jnp.int32)
    inside = degree[None, :] >= wave_own[:, None]
    parity = jnp.where((degree[None, :] + wave_own[:, None]) % 2 == 0, 1.0, -1.0).astype(
        jnp.float32
    )
    masked = jnp.where(inside[:, :, None], spectral, jnp.zeros_like(spectral))
    flipped = jnp.where(parity[:, :, None] > 0, masked, -masked)
    north_half = jnp.einsum("rnj,rnc->jrc", lat_basis, masked, preferred_element_type=jnp.float32)
    south_half = jnp.einsum("rnj,rnc->jrc", lat_basis, flipped, preferred_element_type=jnp.float32)
    fourier = jnp.concatenate([north_half, south_half[::-1]], axis=0).astype(jnp.bfloat16)
    outbound = fourier.reshape(devices, lat_local, row_count, chan_width)
    wave_table = lon_table(wave_all)
    rows_in = lax.all_to_all(outbound, "lat", split_axis=0, concat_axis=2, tiled=True)[0]
    signed = jnp.concatenate([rows_in[:, :, :chan_count], -rows_in[:, :, chan_count:]], axis=1)
    grid_field = jnp.einsum(
        "jrk,rl->jkl", signed, wave_table, preferred_element_type=jnp.float32
    ).astype(jnp.bfloat16)
    weight_own = lat_weights(my_index * lat_local, lat_local, lat_total)
    grid_wide = grid_field.astype(jnp.float32)
    partial_value = jnp.sum(weight_own[:, None, None] * grid_wide * grid_wide, axis=(0, 2))
    global_sum = lax.psum(partial_value, "lat")
    weight_all = lat_weights(0, lat_total, lat_total)
    variance = global_sum / (NLON * jnp.sum(weight_all))
    col_scale = col_gain * lax.rsqrt(variance + 1e-05)
    inv_root = 1.0 / math.sqrt(NLON)
    contract_first = (((0,), (0,)), ((), ()))

    def column(row_grid):
        normed = (row_grid.astype(jnp.float32) * col_scale[:, None]).astype(jnp.bfloat16)
        hidden = jax.nn.gelu(
            lax.dot_general(in_weight, normed, contract_first, preferred_element_type=jnp.float32)
            + in_bias[:, None]
        ).astype(jnp.bfloat16)
        column_out = lax.dot_general(
            out_weight, hidden, contract_first, preferred_element_type=jnp.float32
        ).astype(jnp.bfloat16)
        back_proj = lax.dot_general(
            wave_table, column_out, (((1,), (1,)), ((), ())), preferred_element_type=jnp.float32
        )
        return (
            jnp.concatenate([back_proj[:wave_total], -back_proj[wave_total:]], axis=1) * inv_root
        ).astype(jnp.bfloat16)

    coeffs = lax.map(column, grid_field)
    returning = coeffs.reshape(lat_local, devices, row_count, chan_width)
    factor = 2.0 * math.sqrt(degrees * wave_total / lat_total)
    weighted = (
        weight_all[:, None, None]
        * lax.all_to_all(returning, "lat", split_axis=1, concat_axis=0, tiled=True)[:, 0].astype(
            jnp.float32
        )
    ).astype(jnp.bfloat16)
    north_part = weighted[:half_lat]
    south_part = weighted[half_lat:][::-1]
    east_sum = jnp.einsum("rnj,jrc->rnc", lat_basis, north_part, preferred_element_type=jnp.float32)
    west_sum = jnp.einsum("rnj,jrc->rnc", lat_basis, south_part, preferred_element_type=jnp.float32)
    legendre = factor * (east_sum + parity[:, :, None] * west_sum)
    damp_all = jnp.concatenate([damping, damping])
    wave_factor = (degree * (degree + 1)).astype(jnp.float32) / (NN * NN)
    damped = legendre - damp_all[None, None, :] * wave_factor[None, :, None] * spectral.astype(
        jnp.float32
    )
    return jnp.where(inside[:, :, None], damped, jnp.zeros_like(damped))


def solution(mesh):
    in_specs = (
        P(("member", "lat"), None, None),
        P("lat", None, None),
        P(),
        P(),
        P(),
        P(),
        P(),
        P(),
    )
    out_specs = P(("member", "lat"), None, None)
    return jax.shard_map(
        on_device, mesh=mesh, in_specs=in_specs, out_specs=out_specs, check_vma=False
    )
```

profile of v0, /device:TPU:0, one launch (start us, length us, event | category | flops | bytes accessed | tf_op | source)
XLA Modules:
  0.0 446.9 jit_solution(13777267566337233392)
XLA Ops:
  1.2 6.4 %copy.40 = bf16[16,512,256]{1,2,0:T(8,128)(2,1)} copy(bf16[16,512,256]{2,1,0:T(8,128)(2,1)} %param.10) | data formatting | bytes 8388608 | tf_op args[0]
  7.7 5.0 %fusion.46 = bf16[192,16,256]{2,0,1:T(8,128)(2,1)} fusion(bf16[16,512,192]{1,2,0:T(8,128)(2,1)S(1)} %copy-done, bf16[16,512,256]{1,2,0:T(8,128)(2,1)} %copy.40, pred[16,512]{1,0:T(8,128)(4,1)S(1)} %get-tuple-element.70), kind=kOutput, calls=%fused_computation.61 | convolution fusion | flops 808189952 | bytes 8921088 | tf_op jit(solution)/shard_map/rnj,rnc->jrc/dot_general | solution.py:52
  15.4 29.9 %rev.6 = bf16[192,16,256]{2,0,1:T(8,128)(2,1)} reverse(bf16[192,16,256]{2,0,1:T(8,128)(2,1)} %fusion.42), dimensions={0} | reverse | bytes 3145728 | tf_op jit(solution)/shard_map/rev | solution.py:54
  50.9 7.6 %all-to-all-start = ((bf16[32,12,16,256]{3,2,1,0:T(8,128)(2,1)}), bf16[32,12,16,256]{3,2,1,0:T(8,128)(2,1)}, u32[]{:S(2)}, u32[]{:S(2)}) async-start(bf16[32,12,16,256]{3,2,1,0:T(8,128)(2,1)} %bitcast.68), calls=%async_computation | async-start | bytes 6291456 | tf_op jit(solution)/shard_map/all_to_all | solution.py:57
  59.9 13.5 %cosine_convert_fusion = (bf16[512,1536]{1,0:T(8,128)(2,1)S(1)}, bf16[512,1536]{1,0:T(8,128)(2,1)S(1)}) fusion(s32[512]{0:T(512)S(1)} %fusion.59), kind=kLoop, calls=%fused_computation.50 | loop fusion | flops 8650752 | bytes 3147776 | tf_op jit(solution)/shard_map/convert.4
  77.0 52.9 %all-to-all-done = bf16[32,12,16,256]{3,2,1,0:T(8,128)(2,1)} async-done(((bf16[32,12,16,256]{3,2,1,0:T(8,128)(2,1)}), bf16[32,12,16,256]{3,2,1,0:T(8,128)(2,1)}, u32[]{:S(2)}, u32[]{:S(2)}) %all-to-all-start) | async-done | bytes 3145760 | tf_op jit(solution)/shard_map/all_to_all | solution.py:57
  142.7 10.3 %fusion.25 = (f32[128]{0:T(128)S(1)}, bf16[12,128,1536]{2,1,0:T(8,128)(2,1)}) fusion(f32[12]{0:T(128)S(1)} %multiply_cosine_fusion.1, bf16[512,1536]{1,0:T(8,128)(2,1)} %copy-done.3, bf16[512,1536]{1,0:T(8,128)(2,1)} %copy-done.2, bf16[12,512,128]{1,2,0:T(8,128)(2,1)} %neg.10, bf16[12,512,128]{1,2,0:T(8,128)(2,1)} %copy.56), kind=kOutput, calls=%fused_computation.28 | convolution fusion | flops 4856217600 | bytes 11010608 | tf_op jit(solution)/shard_map/jrk,rl->jkl/dot_general | solution.py:59
  153.0 38.1 %psum.7 = f32[128]{0:T(128)S(1)} all-reduce(f32[128]{0:T(128)S(1)} %get-tuple-element.72), channel_id=1, replica_groups=mesh['member'=1,'lat'=32] {'lat'}, use_global_device_ids=true, to_apply=%region_2.3 | all-reduce | flops 128 | bytes 1024 | tf_op jit(solution)/shard_map/psum | solution.py:65
  191.1 114.6 %while.10 = (s32[]{:T(128)}, bf16[12,512,256]{2,1,0:T(8,128)(2,1)}, bf16[12,128,1536]{2,1,0:T(8,128)(2,1)}, f32[128]{0:T(128)S(1)}, bf16[128,1024]{1,0:T(8,128)(...) while((s32[]{:T(128)}, bf16[12,512,256]{2,1,0:T(8,128)(2,1)}, ...), condition=%wide.region_5.6_spmd, body=%wide.region_4.5_spmd.sunk | while | flops 1224933376 | bytes 8263261 | solution.py:88
  191.1 3.9 convolution_convert_fusion.3
  200.7 3.9 convolution_convert_fusion.3
  210.2 3.9 convolution_convert_fusion.3
  219.8 3.9 convolution_convert_fusion.3
  267.5 3.9 convolution_convert_fusion.3
  277.1 3.9 convolution_convert_fusion.3
  296.2 3.9 convolution_convert_fusion.3
  305.8 4.0 copy.48
  309.7 5.1 %all-to-all-start.1 = ((bf16[12,32,16,256]{3,2,0,1:T(8,128)(2,1)}), bf16[12,32,16,256]{3,2,0,1:T(8,128)(2,1)}, u32[]{:S(2)}, u32[]{:S(2)}) async-start(bf16[12,32,16,256]{3,2,0,1:T(8,128)(2,1)} %copy.48), calls=%async_computation.1 | async-start | bytes 6291456 | tf_op jit(solution)/shard_map/all_to_all | solution.py:93
  316.0 70.4 %all-to-all-done.1 = bf16[12,32,16,256]{3,2,0,1:T(8,128)(2,1)} async-done(((bf16[12,32,16,256]{3,2,0,1:T(8,128)(2,1)}), bf16[12,32,16,256]{3,2,0,1:T(8,128)(2,1)}, u32[]{:S(2)}, u32[]{:S(2)}) %all-to-all-start.1) | async-done | bytes 3145760 | tf_op jit(solution)/shard_map/all_to_all | solution.py:93
  389.1 4.0 fusion.27
  393.0 4.8 %fusion.44 = f32[16,256,512]{2,1,0:T(8,128)} fusion(bf16[16,512,192]{1,2,0:T(8,128)(2,1)S(1)} %copy-done, bf16[384,16,256]{2,0,1:T(8,128)(2,1)S(1)} %fusion.27), kind=kOutput, calls=%fused_computation.59 | convolution fusion | flops 805306368 | bytes 13107200 | tf_op jit(solution)/shard_map/rnj,jrc->rnc/dot_general | solution.py:99
  399.1 29.9 %rev.7 = bf16[192,16,256]{2,0,1:T(8,128)(2,1)} reverse(bf16[192,16,256]{2,0,1:T(8,128)(2,1)} %slice.27), dimensions={0} | reverse | bytes 3145728 | tf_op jit(solution)/shard_map/rev | solution.py:98
  429.0 8.7 %fusion.26 = f32[16,512,256]{1,2,0:T(8,128)} fusion(bf16[16,512,256]{1,2,0:T(8,128)(2,1)} %copy.40, f32[16,256,512]{2,1,0:T(8,128)} %fusion.44, f32[512,256]{0,1:T(8,128)} %broadcast_multiply_fusion, f32[16,512]{1,0:T(8,128)S(1)} %fusion.51, pred[16,512]{1,0:T(8,128)(4,1)S(1)} %get-tuple-element.70, bf16[192,16,256]{2,0,1:T(8,128)(2,1)} %rev.7, ...), kind=kOutput, calls=%fused_computation.30 | convolution fusion | flops 819986432 | bytes 26255360 | tf_op jit(solution)/shard_map/rnj,jrc->rnc/dot_general | solution.py:100
  437.7 9.2 %copy.51 = f32[16,512,256]{2,1,0:T(8,128)} copy(f32[16,512,256]{1,2,0:T(8,128)} %fusion.26) | data formatting | bytes 16777216 | tf_op jit(solution)/shard_map/jit(_where)/select_n | solution.py:107
  (102 shorter events, 118.8 us)
Async XLA Ops:
  0.0 7.7 %copy-start = (bf16[16,512,192]{1,2,0:T(8,128)(2,1)S(1)}, bf16[16,512,192]{1,2,0:T(8,128)(2,1)}, u32[]{:S(2)}) copy-start(bf16[16,512,192]{1,2,0:T(8,128)(2,1)} %param.11) | copy-start | bytes 9437188
  7.7 5.0 %copy-start.1 = (bf16[16,512,256]{1,2,0:T(8,128)(2,1)S(1)}, bf16[16,512,256]{1,2,0:T(8,128)(2,1)}, u32[]{:S(2)}) copy-start(bf16[16,512,256]{1,2,0:T(8,128)(2,1)} %copy.40) | copy-start | bytes 12582916
  50.9 78.9 %all-to-all-start = ((bf16[32,12,16,256]{3,2,1,0:T(8,128)(2,1)}), bf16[32,12,16,256]{3,2,1,0:T(8,128)(2,1)}, u32[]{:S(2)}, u32[]{:S(2)}) async-start(bf16[32,12,16,256]{3,2,1,0:T(8,128)(2,1)} %bitcast.68), calls=%async_computation | async-start | bytes 6291456 | tf_op jit(solution)/shard_map/all_to_all | solution.py:57
  73.4 1.2 copy-start.2
  73.4 1.7 copy-start.3
  142.7 48.4 %copy-start.4 = (f32[128]{0:T(128)S(1)}, f32[128]{0:T(128)}, u32[]{:S(2)}) copy-start(f32[128]{0:T(128)} %param.16) | copy-start | bytes 1540
  309.7 5.2 %copy-start.5 = (f32[128]{0:T(128)S(1)}, f32[128]{0:T(128)}, u32[]{:S(2)}) copy-start(f32[128]{0:T(128)} %param.17) | copy-start | bytes 1540
  309.7 76.6 %all-to-all-start.1 = ((bf16[12,32,16,256]{3,2,0,1:T(8,128)(2,1)}), bf16[12,32,16,256]{3,2,0,1:T(8,128)(2,1)}, u32[]{:S(2)}, u32[]{:S(2)}) async-start(bf16[12,32,16,256]{3,2,0,1:T(8,128)(2,1)} %copy.48), calls=%async_computation.1 | async-start | bytes 6291456 | tf_op jit(solution)/shard_map/all_to_all | solution.py:93
where the time goes:
time: 455 us; the launch traced here: 447 us
  local copies, waits for them, and re-layouts  126 us (28%)
  waiting for transfers between devices  123 us (27%)
  matrix products  115 us (25%)
  blocking collectives  38.1 us (8%)
  other arithmetic  31.1 us (7%)
  starting transfers between devices  12.7 us (3%)
    all_to_all x1, waiting for transfers between devices, on_device(): lax.all_to_all(returning, 'lat', split_axis=1, concat_axis=0, tiled=True)  70.4 us
    all_to_all x1, waiting for transfers between devices, on_device(): lax.all_to_all(outbound, 'lat', split_axis=0, concat_axis=2, tiled=True)[0]  52.9 us
    dot_general x12, matrix products, column(): lax.dot_general(out_weight, hidden, contract_first, preferred_element_typ...  46.7 us
    psum x1, blocking collectives, on_device(): global_sum = lax.psum(partial_value, 'lat')  38.1 us
    dot_general x12, matrix products, column(): lax.dot_general(wave_table, column_out, (((1,), (1,)), ((), ())), preferr...  36.5 us
    dynamic_update_slice x24, local copies, waits for them, and re-layouts, on_device(): coeffs = lax.map(column, grid_field)  30.1 us
    rev x1, local copies, waits for them, and re-layouts, on_device(): south_part = weighted[half_lat:][::-1]  29.9 us
    rev x1, local copies, waits for them, and re-layouts, on_device(): south_half[::-1]  29.9 us
  transfers between devices with their start and end apart: 2, of which 2 were waited for; matrix products, arithmetic and copies ran while one was open for 4% of the time, Pallas kernels for 0%

commit v1 on v0

--- a/solution.py
+++ b/solution.py
@@ -54,7 +54,16 @@
     fourier = jnp.concatenate([north_half, south_half[::-1]], axis=0).astype(jnp.bfloat16)
     outbound = fourier.reshape(devices, lat_local, row_count, chan_width)
     wave_table = lon_table(wave_all)
-    rows_in = lax.all_to_all(outbound, "lat", split_axis=0, concat_axis=2, tiled=True)[0]
+
+    def slots_mix(z_in, row_axis):
+        side_arr = lax.axis_size(row_axis)
+        carry_in = jnp.split(z_in, side_arr, axis=0)
+        met_up = jnp.stack(carry_in, axis=0)
+        opened = lax.all_to_all(met_up, row_axis, 0, 0)
+        block_last = jnp.concatenate(opened, axis=2)
+        return block_last
+
+    rows_in = slots_mix(outbound, row_axis="lat")[0]
     signed = jnp.concatenate([rows_in[:, :, :chan_count], -rows_in[:, :, chan_count:]], axis=1)
     grid_field = jnp.einsum(
         "jrk,rl->jkl", signed, wave_table, preferred_element_type=jnp.float32

time: 455 us -> 490 us (1.077)
  local copies, waits for them, and re-layouts: 126 us -> 164 us
    unnamed x15 -> x46, local copies, waits for them, and re-layouts: 13.3 us -> 48.1 us
    another operation x0 -> x2, local copies, waits for them, and re-layouts: none -> 6.85 us  [slots_mix(): met_up = jnp.stack(carry_in, axis=0)]
where the time goes in v1:
time: 490 us; the launch traced here: 482 us
  local copies, waits for them, and re-layouts  164 us (33%)
  waiting for transfers between devices  123 us (25%)
  matrix products  114 us (23%)
  blocking collectives  38.1 us (8%)
  other arithmetic  28.9 us (6%)
  starting transfers between devices  12.7 us (3%)
    all_to_all x1, waiting for transfers between devices, on_device(): lax.all_to_all(returning, 'lat', split_axis=1, concat_axis=0, tiled=True)  70.4 us
    all_to_all x1, waiting for transfers between devices, slots_mix(): opened = lax.all_to_all(met_up, row_axis, 0, 0)  52.8 us
    unnamed x46, local copies, waits for them, and re-layouts  48.1 us
    dot_general x12, matrix products, column(): lax.dot_general(out_weight, hidden, contract_first, preferred_element_typ...  46.7 us
    psum x1, blocking collectives, on_device(): global_sum = lax.psum(partial_value, 'lat')  38.1 us
    dot_general x12, matrix products, column(): lax.dot_general(wave_table, column_out, (((1,), (1,)), ((), ())), preferr...  36.5 us
    dynamic_update_slice x24, local copies, waits for them, and re-layouts, on_device(): coeffs = lax.map(column, grid_field)  30.1 us
    rev x1, local copies, waits for them, and re-layouts, on_device(): south_part = weighted[half_lat:][::-1]  29.9 us
  transfers between devices with their start and end apart: 2, of which 2 were waited for; matrix products, arithmetic and copies ran while one was open for 4% of the time, Pallas kernels for 0%

profile of v1, /device:TPU:0, one launch (start us, length us, event | category | flops | bytes accessed | tf_op | source)
XLA Modules:
  0.0 481.7 jit_solution(4249654012387218475)
XLA Ops:
  1.2 6.4 %copy.49 = bf16[16,512,256]{1,2,0:T(8,128)(2,1)} copy(bf16[16,512,256]{2,1,0:T(8,128)(2,1)} %param.10) | data formatting | bytes 8388608 | tf_op args[0]
  25.1 29.8 %rev.6 = bf16[192,16,256]{2,0,1:T(8,128)(2,1)} reverse(bf16[192,16,256]{2,0,1:T(8,128)(2,1)} %fusion.42), dimensions={0} | reverse | bytes 3145728 | tf_op jit(solution)/shard_map/rev | solution.py:54
  80.5 5.3 %copy.52 = bf16[32,1,12,16,256]{4,3,2,1,0:T(8,128)(2,1)} copy(bf16[32,1,12,16,256]{4,2,3,1,0:T(8,128)(2,1)} %fusion.47) | data formatting | bytes 6291456 | tf_op jit(solution)/shard_map/stack | solution.py:61
  85.7 7.6 %all-to-all-start = ((bf16[32,1,12,16,256]{4,3,2,1,0:T(8,128)(2,1)}), bf16[32,1,12,16,256]{4,3,2,1,0:T(8,128)(2,1)}, u32[]{:S(2)}, u32[]{:S(2)}) async-start(bf16[32,1,12,16,256]{4,3,2,1,0:T(8,128)(2,1)} %copy.52), calls=%async_computation | async-start | bytes 6291456 | tf_op jit(solution)/shard_map/all_to_all | solution.py:62
  94.7 13.5 %cosine_convert_fusion = (bf16[512,1536]{1,0:T(8,128)(2,1)S(1)}, bf16[512,1536]{1,0:T(8,128)(2,1)S(1)}) fusion(s32[512]{0:T(512)S(1)} %fusion.91), kind=kLoop, calls=%fused_computation.49 | loop fusion | flops 8650752 | bytes 3147776 | tf_op jit(solution)/shard_map/convert.4
  111.8 52.8 %all-to-all-done = bf16[32,1,12,16,256]{4,3,2,1,0:T(8,128)(2,1)} async-done(((bf16[32,1,12,16,256]{4,3,2,1,0:T(8,128)(2,1)}), bf16[32,1,12,16,256]{4,3,2,1,0:T(8,128)(2,1)}, u32[]{:S(2)}, u32[]{:S(2)}) %all-to-all-start) | async-done | bytes 3145760 | tf_op jit(solution)/shard_map/all_to_all | solution.py:62
  177.5 10.3 %fusion.25 = (f32[128]{0:T(128)S(1)}, bf16[12,128,1536]{2,1,0:T(8,128)(2,1)}) fusion(f32[12]{0:T(128)S(1)} %multiply_cosine_fusion.1, bf16[512,1536]{1,0:T(8,128)(2,1)} %copy-done.3, bf16[512,1536]{1,0:T(8,128)(2,1)} %copy-done.2, bf16[12,512,128]{1,2,0:T(8,128)(2,1)} %neg.10, bf16[12,512,128]{1,2,0:T(8,128)(2,1)} %copy.65), kind=kOutput, calls=%fused_computation.28 | convolution fusion | flops 4856217600 | bytes 11010608 | tf_op jit(solution)/shard_map/jrk,rl->jkl/dot_general | solution.py:68
  187.8 38.1 %psum.7 = f32[128]{0:T(128)S(1)} all-reduce(f32[128]{0:T(128)S(1)} %get-tuple-element.72), channel_id=1, replica_groups=mesh['member'=1,'lat'=32] {'lat'}, use_global_device_ids=true, to_apply=%region_2.3 | all-reduce | flops 128 | bytes 1024 | tf_op jit(solution)/shard_map/psum | solution.py:74
  225.9 114.6 %while.10 = (s32[]{:T(128)}, bf16[12,512,256]{2,1,0:T(8,128)(2,1)}, bf16[12,128,1536]{2,1,0:T(8,128)(2,1)}, f32[128]{0:T(128)S(1)}, bf16[128,1024]{1,0:T(8,128)(...) while((s32[]{:T(128)}, bf16[12,512,256]{2,1,0:T(8,128)(2,1)}, ...), condition=%wide.region_5.6_spmd, body=%wide.region_4.5_spmd.sunk | while | flops 1224933376 | bytes 8263261 | solution.py:97
  225.9 3.9 convolution_convert_fusion.3
  235.5 3.9 convolution_convert_fusion.3
  254.6 3.9 convolution_convert_fusion.3
  273.7 3.9 convolution_convert_fusion.3
  302.3 3.9 convolution_convert_fusion.3
  311.9 3.9 convolution_convert_fusion.3
  331.0 3.9 convolution_convert_fusion.3
  340.6 4.0 copy.57
  344.5 5.1 %all-to-all-start.1 = ((bf16[12,32,16,256]{3,2,0,1:T(8,128)(2,1)}), bf16[12,32,16,256]{3,2,0,1:T(8,128)(2,1)}, u32[]{:S(2)}, u32[]{:S(2)}) async-start(bf16[12,32,16,256]{3,2,0,1:T(8,128)(2,1)} %copy.57), calls=%async_computation.1 | async-start | bytes 6291456 | tf_op jit(solution)/shard_map/all_to_all | solution.py:102
  350.8 70.4 %all-to-all-done.1 = bf16[12,32,16,256]{3,2,0,1:T(8,128)(2,1)} async-done(((bf16[12,32,16,256]{3,2,0,1:T(8,128)(2,1)}), bf16[12,32,16,256]{3,2,0,1:T(8,128)(2,1)}, u32[]{:S(2)}, u32[]{:S(2)}) %all-to-all-start.1) | async-done | bytes 3145760 | tf_op jit(solution)/shard_map/all_to_all | solution.py:102
  423.9 4.0 fusion.27
  427.8 4.8 fusion.44
  433.9 29.9 %rev.7 = bf16[192,16,256]{2,0,1:T(8,128)(2,1)} reverse(bf16[192,16,256]{2,0,1:T(8,128)(2,1)} %slice.91), dimensions={0} | reverse | bytes 3145728 | tf_op jit(solution)/shard_map/rev | solution.py:107
  463.8 8.7 %fusion.26 = f32[16,512,256]{1,2,0:T(8,128)} fusion(bf16[16,512,256]{1,2,0:T(8,128)(2,1)} %copy.49, f32[16,256,512]{2,1,0:T(8,128)} %fusion.44, f32[512,256]{0,1:T(8,128)} %broadcast_multiply_fusion, f32[16,512]{1,0:T(8,128)S(1)} %fusion.83, pred[16,512]{1,0:T(8,128)(4,1)S(1)} %get-tuple-element.71, bf16[192,16,256]{2,0,1:T(8,128)(2,1)} %rev.7, ...), kind=kOutput, calls=%fused_computation.30 | convolution fusion | flops 819986432 | bytes 26255360 | tf_op jit(solution)/shard_map/rnj,jrc->rnc/dot_general | solution.py:109
  472.4 9.2 %copy.60 = f32[16,512,256]{2,1,0:T(8,128)} copy(f32[16,512,256]{1,2,0:T(8,128)} %fusion.26) | data formatting | bytes 16777216 | tf_op jit(solution)/shard_map/jit(_where)/select_n | solution.py:116
  (133 shorter events, 153.3 us)
Async XLA Ops:
  0.0 7.7 %copy-start = (bf16[16,512,192]{1,2,0:T(8,128)(2,1)S(1)}, bf16[16,512,192]{1,2,0:T(8,128)(2,1)}, u32[]{:S(2)}) copy-start(bf16[16,512,192]{1,2,0:T(8,128)(2,1)} %param.11) | copy-start | bytes 9437188
  11.4 10.9 %copy-start.1 = (bf16[16,512,256]{1,2,0:T(8,128)(2,1)S(1)}, bf16[16,512,256]{1,2,0:T(8,128)(2,1)}, u32[]{:S(2)}) copy-start(bf16[16,512,256]{1,2,0:T(8,128)(2,1)} %copy.49) | copy-start | bytes 12582916
  85.7 78.9 %all-to-all-start = ((bf16[32,1,12,16,256]{4,3,2,1,0:T(8,128)(2,1)}), bf16[32,1,12,16,256]{4,3,2,1,0:T(8,128)(2,1)}, u32[]{:S(2)}, u32[]{:S(2)}) async-start(bf16[32,1,12,16,256]{4,3,2,1,0:T(8,128)(2,1)} %copy.52), calls=%async_computation | async-start | bytes 6291456 | tf_op jit(solution)/shard_map/all_to_all | solution.py:62
  108.2 1.2 copy-start.2
  108.2 1.7 copy-start.3
  177.5 48.4 %copy-start.4 = (f32[128]{0:T(128)S(1)}, f32[128]{0:T(128)}, u32[]{:S(2)}) copy-start(f32[128]{0:T(128)} %param.16) | copy-start | bytes 1540
  344.5 5.1 %copy-start.5 = (f32[128]{0:T(128)S(1)}, f32[128]{0:T(128)}, u32[]{:S(2)}) copy-start(f32[128]{0:T(128)} %param.17) | copy-start | bytes 1540
  344.5 76.6 %all-to-all-start.1 = ((bf16[12,32,16,256]{3,2,0,1:T(8,128)(2,1)}), bf16[12,32,16,256]{3,2,0,1:T(8,128)(2,1)}, u32[]{:S(2)}, u32[]{:S(2)}) async-start(bf16[12,32,16,256]{3,2,0,1:T(8,128)(2,1)} %copy.57), calls=%async_computation.1 | async-start | bytes 6291456 | tf_op jit(solution)/shard_map/all_to_all | solution.py:102
